TPU v7x, 512 devices: a whole 4x8x8 slice. The times are simulated.
512 devices in a mesh: rows: 64 (over z, y), feat: 8 (over x, core).
Axes of the slice: x: 4, y: 8, z: 8, core: 2. Of those that a mesh axis runs over, the one named last changes fastest.
Arguments:
- node_feats: bfloat16 [65536, 256], P('rows', 'feat'), may hold values from -6 to 6
- band_weights: bfloat16 [65536, 384], P('rows'), may hold values from 0 to 1.5, as said below
- far_weights: bfloat16 [65536, 256], P('rows'), may hold values from 0 to 1.5, as said below
- far_owner: int32 [512, 2], P('rows'), may hold values from 0 to 63, all different within a row; in each aligned block of 8 rows (0 to 7, 8 to 15, ...) at most 2 rows name the same one
- far_local: int32 [512, 2], P('rows'), may hold values from 0 to 7
- w_self: bfloat16 [256, 256], replicated, may hold values from -0.375 to 0.375
- w_neigh: bfloat16 [256, 256], replicated, may hold values from -0.375 to 0.375
- bias: float32 [256], P('feat'), may hold values from -3 to 3
- cotangent: bfloat16 [65536, 256], P('rows', 'feat'), may hold values from -16 to 16
Outputs:
- layer_out: bfloat16 [65536, 256], P('rows', 'feat')
- grad_feats: float32 [65536, 256], P('rows', 'feat')
- grad_self: float32 [256, 256], P('feat')
- grad_neigh: float32 [256, 256], P('feat')
Inputs may be any that keep to these rules, and one draw needn't show every extreme that they name: `far_owner`: among the far entries of the 8 row blocks of one device, no owner is named more than 2 times, and in every draw some owner is named exactly 2 times in some device's blocks; the 2 owners of one row block differ. `band_weights`: each row has a positive weight on the node's own entry of its own block; other entries are zero or positive. `far_weights`: entries are zero or positive.
All inputs are finite; a program needn't handle non-finite values.
Results may differ from a plain program's by a relative error of at most 0.0049.
Values may be sent and summed in bfloat16 or wider, within the bound.
No kernel may reach another device: no remote copies, remote signals or barrier semaphores. Data moves between devices by JAX's collectives and lax.ppermute only.
A program may use at most 64 MiB of HBM per device.

v0:
```python
import jax
import jax.numpy as jnp
from jax import lax
from jax.sharding import PartitionSpec as P


def extended(block, sides, width):
    for axis, dim in sides:
        count = lax.axis_size(axis)
        forward = [(i, i + 1) for i in range(count - 1)]
        backward = [(target, source) for source, target in forward]
        low = lax.ppermute(
            lax.slice_in_dim(block, block.shape[dim] - width, None, axis=dim), axis, forward
        )
        high = lax.ppermute(lax.slice_in_dim(block, 0, width, axis=dim), axis, backward)
        block = jnp.concatenate([low, block, high], axis=dim)
    return block


def from_behind(block, axis, distance):
    devices = range(lax.axis_size(axis))
    route = [(i - distance, i) for i in devices if i - distance in devices]
    return lax.ppermute(block, axis, route)


def on_device(
    node_feats, band_weights, far_weights, far_owner, far_local, w_self, w_neigh, bias, cotangent
):
    rows_dev, col_count = node_feats.shape
    tile_size = band_weights.shape[1] // 3
    blocks = rows_dev // tile_size
    fanout = far_owner.shape[1]
    peer_count = lax.axis_size("rows")
    capacity = max(2, 2 * blocks * fanout // peer_count)
    col_start = lax.axis_index("feat") * col_count
    bias_high = lax.reduce_precision(bias, exponent_bits=8, mantissa_bits=7)
    bias_rest = bias - bias_high
    bias_mid = lax.reduce_precision(bias_rest, exponent_bits=8, mantissa_bits=7)
    bias_parts = jnp.zeros((16, col_count), jnp.bfloat16)
    bias_parts = bias_parts.at[:3].set(
        jnp.stack([bias_high, bias_mid, bias_rest - bias_mid]).astype(jnp.bfloat16)
    )
    packed = jnp.concatenate([node_feats, cotangent, bias_parts], axis=0)
    gathered = lax.all_gather(packed, "feat", axis=1, tiled=True)
    feats_all = gathered[:rows_dev]
    cotangent_all = gathered[rows_dev : 2 * rows_dev]
    bias_rows = gathered[2 * rows_dev : 2 * rows_dev + 3].astype(jnp.float32)
    bias_all = bias_rows[0] + bias_rows[1] + bias_rows[2]
    padded = extended(node_feats, (("rows", 0),), tile_size)
    windows = jnp.concatenate(
        [
            padded[offset * tile_size : offset * tile_size + rows_dev].reshape(
                blocks, tile_size, col_count
            )
            for offset in range(3)
        ],
        axis=1,
    )
    band_tiles = band_weights.reshape(blocks, tile_size, 3 * tile_size)
    band_sum = jnp.einsum("bij,bjc->bic", band_tiles, windows, preferred_element_type=jnp.float32)
    owner_ids = far_owner.reshape(-1)
    local_ids = far_local.reshape(-1)
    entries = owner_ids.shape[0]
    same_owner = owner_ids[:, None] == owner_ids[None, :]
    earlier = jnp.arange(entries)[None, :] < jnp.arange(entries)[:, None]
    slot_rank = jnp.sum(jnp.where(same_owner & earlier, 1, 0), axis=1).astype(jnp.int32)
    slot_ids = owner_ids * capacity + slot_rank
    slot_hit = slot_ids[:, None] == jnp.arange(peer_count * capacity, dtype=jnp.int32)[None, :]
    request = (jnp.sum(jnp.where(slot_hit, local_ids[:, None] + 1, 0), axis=0) - 1).reshape(
        peer_count, capacity
    )
    wanted = lax.all_to_all(request, "rows", split_axis=0, concat_axis=0, tiled=True)
    usable = wanted >= 0
    safe_ids = jnp.maximum(wanted, 0)
    own_blocks = node_feats.reshape(blocks, tile_size, col_count)
    outgoing = jnp.where(
        usable[:, :, None, None], own_blocks[safe_ids], jnp.zeros((), jnp.bfloat16)
    )
    incoming = lax.all_to_all(outgoing, "rows", split_axis=0, concat_axis=0, tiled=True)
    fetched = incoming.reshape(peer_count * capacity, tile_size, col_count)[slot_ids].reshape(
        blocks, fanout * tile_size, col_count
    )
    far_tiles = far_weights.reshape(blocks, tile_size, fanout * tile_size)
    far_sum = jnp.einsum("bij,bjc->bic", far_tiles, fetched, preferred_element_type=jnp.float32)
    degree = jnp.sum(band_weights.astype(jnp.float32), axis=1) + jnp.sum(
        far_weights.astype(jnp.float32), axis=1
    )
    neighbours = ((band_sum + far_sum).reshape(rows_dev, col_count) / degree[:, None]).astype(
        jnp.bfloat16
    )
    rows_self = lax.dynamic_slice_in_dim(w_self, col_start, col_count, 0)
    rows_neigh = lax.dynamic_slice_in_dim(w_neigh, col_start, col_count, 0)
    neighbours_all = lax.all_gather(neighbours, "feat", axis=1, tiled=True)
    preact_all = (
        jnp.dot(feats_all, w_self, preferred_element_type=jnp.float32)
        + jnp.dot(neighbours_all, w_neigh, preferred_element_type=jnp.float32)
        + bias_all
    )
    preact = lax.dynamic_slice_in_dim(preact_all, col_start, col_count, 1)
    layer_out = jax.nn.silu(preact).astype(jnp.bfloat16)
    sigmoid_z = jax.nn.sigmoid(preact_all)
    full_grad = (
        cotangent_all.astype(jnp.float32) * sigmoid_z * (1.0 + preact_all * (1.0 - sigmoid_z))
    ).astype(jnp.bfloat16)
    grad_scale = float(rows_dev * peer_count) ** (-0.5)
    part_self = jnp.einsum("rc,rf->cf", node_feats, full_grad, preferred_element_type=jnp.float32)
    part_neigh = jnp.einsum("rc,rf->cf", neighbours, full_grad, preferred_element_type=jnp.float32)
    dense_grad = jnp.einsum("rf,cf->rc", full_grad, rows_self, preferred_element_type=jnp.float32)
    grad_agg = jnp.einsum("rf,cf->rc", full_grad, rows_neigh, preferred_element_type=jnp.float32)
    grad_neighbours = (grad_agg / degree[:, None]).astype(jnp.bfloat16)
    grad_blocks = grad_neighbours.reshape(blocks, tile_size, col_count)
    grad_windows = jnp.einsum(
        "bij,bic->bjc", band_tiles, grad_blocks, preferred_element_type=jnp.float32
    )
    grad_padded = jnp.zeros((rows_dev + 2 * tile_size, col_count), jnp.float32)
    for offset in range(3):
        piece = grad_windows[:, offset * tile_size : (offset + 1) * tile_size, :].reshape(
            rows_dev, col_count
        )
        grad_padded = grad_padded + jnp.pad(
            piece, ((offset * tile_size, (2 - offset) * tile_size), (0, 0))
        )
    top_rim = grad_padded[:tile_size]
    bottom_rim = grad_padded[rows_dev + tile_size :]
    from_below = from_behind(top_rim, "rows", -1)
    from_above = from_behind(bottom_rim, "rows", 1)
    grad_fetched = jnp.einsum(
        "bij,bic->bjc", far_tiles, grad_blocks, preferred_element_type=jnp.float32
    )
    returning = jnp.zeros((peer_count * capacity, tile_size, col_count), jnp.float32)
    returning = returning.at[slot_ids].set(grad_fetched.reshape(entries, tile_size, col_count))
    feat_count = lax.axis_size("feat")
    feat_index = lax.axis_index("feat")
    slotted = jnp.zeros((2, feat_count, col_count, feat_count * col_count), jnp.float32)
    slotted = lax.dynamic_update_index_in_dim(
        slotted, jnp.stack([part_self, part_neigh])[:, None], feat_index, 1
    )
    summed = lax.psum(slotted, ("rows", "feat"))
    sum_self, sum_neigh = lax.dynamic_index_in_dim(summed, feat_index, 1, keepdims=False)
    grad_self = sum_self * grad_scale
    grad_neigh = sum_neigh * grad_scale
    returned = lax.all_to_all(
        returning.reshape(peer_count, capacity, tile_size, col_count).astype(jnp.bfloat16),
        "rows",
        split_axis=0,
        concat_axis=0,
        tiled=True,
    ).astype(jnp.float32)
    target_block = jnp.where(usable, wanted, blocks).reshape(-1)
    owed = jnp.zeros((blocks, tile_size * col_count), jnp.float32)
    owed = owed.at[target_block].add(
        returned.reshape(peer_count * capacity, tile_size * col_count), mode="drop"
    )
    interior = (
        dense_grad
        + grad_padded[tile_size : tile_size + rows_dev]
        + owed.reshape(rows_dev, col_count)
    )
    interior = interior.at[:tile_size].add(from_above)
    grad_feats = interior.at[rows_dev - tile_size :].add(from_below)
    return (layer_out, grad_feats, grad_self, grad_neigh)


def solution(mesh):
    in_specs = (
        P("rows", "feat"),
        P("rows", None),
        P("rows", None),
        P("rows", None),
        P("rows", None),
        P(),
        P(),
        P("feat"),
        P("rows", "feat"),
    )
    out_specs = (P("rows", "feat"), P("rows", "feat"), P("feat", None), P("feat", None))
    return jax.shard_map(
        on_device, mesh=mesh, in_specs=in_specs, out_specs=out_specs, check_vma=False
    )
```

profile of v0, /device:TPU:24, one launch (start us, length us, event | category | flops | bytes accessed | tf_op | source)
XLA Modules:
  0.0 413.4 jit_solution(3449586873717167894)
XLA Ops:
  8.0 1.5 fusion.14
  10.4 0.8 copy.103
  11.6 0.8 sub.18
  12.3 16.4 %all-to-all-start = ((s32[64,1,2]{2,1,0:T(1,128)}), s32[64,1,2]{2,1,0:T(1,128)S(1)}, u32[]{:S(2)}, u32[]{:S(2)}) async-start(s32[64,1,2]{2,1,0:T(1,128)} %bitcast.4), calls=%async_computation | async-start | bytes 65536 | tf_op jit(solution)/shard_map/all_to_all | solution.py:72
  28.7 0.9 copy_bitcast_fusion.4
  29.6 8.4 %all-to-all-done = s32[64,1,2]{2,1,0:T(1,128)S(1)} async-done(((s32[64,1,2]{2,1,0:T(1,128)}), s32[64,1,2]{2,1,0:T(1,128)S(1)}, u32[]{:S(2)}, u32[]{:S(2)}) %all-to-all-start) | async-done | bytes 544 | tf_op jit(solution)/shard_map/all_to_all | solution.py:72
  38.4 0.8 fusion.43
  39.7 0.8 gather_fusion
  40.5 1.2 broadcast_select_fusion
  41.7 7.3 %all-to-all-start.1 = ((bf16[64,2,128,32]{2,3,1,0:T(8,128)(2,1)}), bf16[64,2,128,32]{2,3,1,0:T(8,128)(2,1)S(1)}, u32[]{:S(2)}, u32[]{:S(2)}) async-start(bf16[64,2,128,32]{2,3,1,0:T(8,128)(2,1)} %broadcast_select_fusion), calls=%async_computation.1 | async-start | bytes 2097152 | tf_op jit(solution)/shard_map/all_to_all | solution.py:79
  49.0 4.7 %collective-permute-start = (bf16[128,32]{0,1:T(8,128)(2,1)S(1)}, bf16[128,32]{0,1:T(8,128)(2,1)S(1)}, u32[]{:S(2)}, u32[]{:S(2)}) collective-permute-start(bf16[128,32]{0,1:T(8,128)(2,1)S(1)} %get-tuple-element.51), channel_id=1, source_target_pairs={{0,8},{8,16},{16,24},{24,32},{32,40},{40,48},{48,56},{56,64},{64,7... | collective-permute-start | bytes 24584 | tf_op jit(solution)/shard_map/ppermute | solution.py:12
  53.8 1.9 collective-permute-start.1
  56.4 14.6 %collective-permute-done = bf16[128,32]{0,1:T(8,128)(2,1)S(1)} collective-permute-done((bf16[128,32]{0,1:T(8,128)(2,1)S(1)}, bf16[128,32]{0,1:T(8,128)(2,1)S(1)}, u32[]{:S(2)}, u32[]{:S(2)}) %collective-permute-start) | collective-permute-done | bytes 8224 | tf_op jit(solution)/shard_map/ppermute | solution.py:12
  71.0 2.1 collective-permute-done.1
  73.6 0.9 slice_convert_fusion
  74.6 2.4 fusion.5
  78.4 13.4 %all_gather.7 = bf16[1024,256]{0,1:T(8,128)(2,1)S(1)} all-gather(bf16[1024,32]{0,1:T(8,128)(2,1)S(1)} %fusion.15), channel_id=1, replica_groups=mesh['rows'=64,'feat'=8] {'feat'}, dimensions={1}, use_global_device_ids=true | all-gather | bytes 589824 | tf_op jit(solution)/shard_map/all_gather | solution.py:93
  91.9 2.7 multiply_convert_fusion
  95.9 1.0 scatter_fusion
  97.0 1.2 convert_element_type.46
  98.2 10.4 %all-to-all-start.2 = ((bf16[64,2,128,32]{2,3,1,0:T(8,128)(2,1)}), bf16[64,2,128,32]{2,3,1,0:T(8,128)(2,1)S(1)}, u32[]{:S(2)}, u32[]{:S(2)}) async-start(bf16[64,2,128,32]{2,3,1,0:T(8,128)(2,1)} %bitcast.107), calls=%async_computation.2 | async-start | bytes 2097152 | tf_op jit(solution)/shard_map/all_to_all | solution.py:142
  110.3 0.8 copy-done.5
  111.1 1.6 multiply_convert_fusion.1
  113.3 4.6 %collective-permute-start.2 = (f32[128,32]{0,1:T(8,128)}, f32[128,32]{0,1:T(8,128)}, u32[]{:S(2)}, u32[]{:S(2)}) collective-permute-start(f32[128,32]{0,1:T(8,128)} %get-tuple-element.45), channel_id=1, source_target_pairs={{0,8},{8,16},{16,24},{24,32},{32,40},{40,48},{48,56},{56,64},{64,7... | collective-permute-start | bytes 49160 | tf_op jit(solution)/shard_map/ppermute | solution.py:23
  117.9 2.1 collective-permute-start.3
  120.7 266.5 %all-reduce.6.cloned.1.call-done = f32[2,8,32,256]{3,2,1,0:T(8,128)} async-done(((f32[2,8,32,256]{3,2,1,0:T(8,128)}), f32[2,8,32,256]{3,2,1,0:T(8,128)}) %all-reduce.6.cloned.1.call-update) | async-done | bytes 524304 | tf_op jit(solution)/shard_map/psum | solution.py:138
  387.2 1.4 fusion.27
  388.6 4.1 copy.120
  392.7 6.3 %reshape.303 = f32[128,4096]{1,0:T(8,128)S(1)} reshape(f32[64,2,128,32]{3,2,1,0:T(8,128)} %copy.120) | data formatting | bytes 4194304 | tf_op jit(solution)/shard_map/reshape | solution.py:152
  399.0 4.0 scatter_custom_fusion.1
  402.9 1.1 reshape.272
  404.2 0.9 fusion.1
  (89 shorter events, 11.6 us)
Async XLA Ops:
  7.2 84.7 %copy-start = (bf16[256,256]{1,0:T(8,128)(2,1)S(1)}, bf16[256,256]{1,0:T(8,128)(2,1)}, u32[]{:S(2)}) copy-start(bf16[256,256]{1,0:T(8,128)(2,1)} %param.21) | copy-start | bytes 393220
  7.2 66.4 %all-gather.2.cloned.1.call-start = ((), (), s32[]{:S(2)}) async-start(), calls=%async_computation.3 | async-start | bytes 1253376 | tf_op jit(solution)/shard_map/all_gather | solution.py:44
  12.3 25.6 %all-to-all-start = ((s32[64,1,2]{2,1,0:T(1,128)}), s32[64,1,2]{2,1,0:T(1,128)S(1)}, u32[]{:S(2)}, u32[]{:S(2)}) async-start(s32[64,1,2]{2,1,0:T(1,128)} %bitcast.4), calls=%async_computation | async-start | bytes 65536 | tf_op jit(solution)/shard_map/all_to_all | solution.py:72
  40.4 8.5 %copy-start.6 = (bf16[1024,32]{0,1:T(8,128)(2,1)S(1)}, bf16[1024,32]{0,1:T(8,128)(2,1)}, u32[]{:S(2)}) copy-start(bf16[1024,32]{0,1:T(8,128)(2,1)} %param.15) | copy-start | bytes 196612
  40.5 15.2 %copy-start.11 = (s32[8,2]{0,1:T(2,128)S(1)}, s32[8,2]{0,1:T(2,128)}, u32[]{:S(2)}) copy-start(s32[8,2]{0,1:T(2,128)} %param.18) | copy-start | bytes 196
  40.5 15.4 %copy-start.2 = (bf16[1024,256]{1,0:T(8,128)(2,1)S(1)}, bf16[1024,256]{1,0:T(8,128)(2,1)}, u32[]{:S(2)}) copy-start(bf16[1024,256]{1,0:T(8,128)(2,1)} %param.17) | copy-start | bytes 1572868
  40.5 15.6 %copy-start.1 = (bf16[1024,384]{1,0:T(8,128)(2,1)S(1)}, bf16[1024,384]{1,0:T(8,128)(2,1)}, u32[]{:S(2)}) copy-start(bf16[1024,384]{1,0:T(8,128)(2,1)} %param.16) | copy-start | bytes 2359300
  41.7 35.7 %all-to-all-start.1 = ((bf16[64,2,128,32]{2,3,1,0:T(8,128)(2,1)}), bf16[64,2,128,32]{2,3,1,0:T(8,128)(2,1)S(1)}, u32[]{:S(2)}, u32[]{:S(2)}) async-start(bf16[64,2,128,32]{2,3,1,0:T(8,128)(2,1)} %broadcast_select_fusion), calls=%async_computation.1 | async-start | bytes 2097152 | tf_op jit(solution)/shard_map/all_to_all | solution.py:79
  49.0 25.6 %copy-start.10 = (bf16[256,256]{1,0:T(8,128)(2,1)S(1)}, bf16[256,256]{1,0:T(8,128)(2,1)}, u32[]{:S(2)}) copy-start(bf16[256,256]{1,0:T(8,128)(2,1)} %param.20) | copy-start | bytes 393220
  49.0 21.9 %collective-permute-start = (bf16[128,32]{0,1:T(8,128)(2,1)S(1)}, bf16[128,32]{0,1:T(8,128)(2,1)S(1)}, u32[]{:S(2)}, u32[]{:S(2)}) collective-permute-start(bf16[128,32]{0,1:T(8,128)(2,1)S(1)} %get-tuple-element.51), channel_id=1, source_target_pairs={{0,8},{8,16},{16,24},{24,32},{32,40},{40,48},{48,56},{56,64},{64,7... | collective-permute-start | bytes 24584 | tf_op jit(solution)/shard_map/ppermute | solution.py:12
  53.8 19.3 %collective-permute-start.1 = (bf16[128,32]{0,1:T(8,128)(2,1)S(1)}, bf16[128,32]{0,1:T(8,128)(2,1)S(1)}, u32[]{:S(2)}, u32[]{:S(2)}) collective-permute-start(bf16[128,32]{0,1:T(8,128)(2,1)S(1)} %get-tuple-element.52), channel_id=1, source_target_pairs={{8,0},{16,8},{24,16},{32,24},{40,32},{48,40},{56,48},{64,56},{72,6... | collective-permute-start | bytes 24584 | tf_op jit(solution)/shard_map/ppermute | solution.py:15
  78.0 13.9 %copy-start.7 = (f32[1024,256]{0,1:T(8,128)S(1)}, f32[1024,256]{0,1:T(8,128)}, u32[]{:S(2)}) copy-start(f32[1024,256]{0,1:T(8,128)} %fusion.5) | copy-start | bytes 3145732
  94.6 0.8 copy-start.3
  98.2 11.5 %copy-start.4 = (bf16[1024,256]{0,1:T(8,128)(2,1)S(1)}, bf16[1024,256]{0,1:T(8,128)(2,1)}, u32[]{:S(2)}) copy-start(bf16[1024,256]{0,1:T(8,128)(2,1)} %copy-done.3) | copy-start | bytes 1572868
  98.2 290.5 %all-to-all-start.2 = ((bf16[64,2,128,32]{2,3,1,0:T(8,128)(2,1)}), bf16[64,2,128,32]{2,3,1,0:T(8,128)(2,1)S(1)}, u32[]{:S(2)}, u32[]{:S(2)}) async-start(bf16[64,2,128,32]{2,3,1,0:T(8,128)(2,1)} %bitcast.107), calls=%async_computation.2 | async-start | bytes 2097152 | tf_op jit(solution)/shard_map/all_to_all | solution.py:142
  108.6 278.7 %all-reduce.6.cloned.1.call-start = ((), (), s32[]{:S(2)}) async-start(), calls=%async_computation.4 | async-start | bytes 1048576 | tf_op jit(solution)/shard_map/psum | solution.py:138
  110.3 0.8 copy-start.5
  113.3 291.8 %collective-permute-start.2 = (f32[128,32]{0,1:T(8,128)}, f32[128,32]{0,1:T(8,128)}, u32[]{:S(2)}, u32[]{:S(2)}) collective-permute-start(f32[128,32]{0,1:T(8,128)} %get-tuple-element.45), channel_id=1, source_target_pairs={{0,8},{8,16},{16,24},{24,32},{32,40},{40,48},{48,56},{56,64},{64,7... | collective-permute-start | bytes 49160 | tf_op jit(solution)/shard_map/ppermute | solution.py:23
  117.9 287.9 %collective-permute-start.3 = (f32[128,32]{0,1:T(8,128)}, f32[128,32]{0,1:T(8,128)S(1)}, u32[]{:S(2)}, u32[]{:S(2)}) collective-permute-start(f32[128,32]{0,1:T(8,128)} %get-tuple-element.44), channel_id=1, source_target_pairs={{8,0},{16,8},{24,16},{32,24},{40,32},{48,40},{56,48},{64,56},{72,6... | collective-permute-start | bytes 49160 | tf_op jit(solution)/shard_map/ppermute | solution.py:23
  392.7 11.5 %copy-start.8 = (f32[1280,32]{0,1:T(8,128)S(1)}, f32[1280,32]{0,1:T(8,128)}, u32[]{:S(2)}) copy-start(f32[1280,32]{0,1:T(8,128)} %pad_add_fusion) | copy-start | bytes 491524
  405.9 0.7 copy-start.9
Sparse Core Ops, SparseCore 0:
  10.1 33.2 all-gather.1
  114.4 272.7 all-reduce.5
where the time goes:
time: 414 us; the launch traced here: 413 us
  waiting for transfers between devices  292 us (71%)
  starting transfers between devices  47.4 us (11%)
  local copies, waits for them, and re-layouts  20.5 us (5%)
  other arithmetic  17.6 us (4%)
  between operations  14.5 us (4%)
  blocking collectives  13.4 us (3%)
  matrix products  7.76 us (2%)
    psum x1, waiting for transfers between devices, on_device(): summed = lax.psum(slotted, ('rows', 'feat'))  267 us
    all_to_all x1, starting transfers between devices, on_device(): lax.all_to_all(request, 'rows', split_axis=0, concat_axis=0, tiled=True)  16.4 us
    ppermute x1, waiting for transfers between devices, extended(): lax.ppermute(lax.slice_in_dim(block, block.shape[dim] - width, None, axis...  14.6 us
    all_gather x1, blocking collectives, on_device(): neighbours_all = lax.all_gather(neighbours, 'feat', axis=1, tiled=True)  13.4 us
    all_to_all x1, starting transfers between devices, on_device(): lax.all_to_all(returning.reshape(peer_count, capacity, tile_size, col_cou...  10.4 us
    reshape x2, local copies, waits for them, and re-layouts, on_device(): returned.reshape(peer_count * capacity, tile_size * col_count)  10.3 us
    all_to_all x1, waiting for transfers between devices, on_device(): lax.all_to_all(request, 'rows', split_axis=0, concat_axis=0, tiled=True)  8.37 us
  transfers between devices with their start and end apart: 9, of which 5 were waited for; matrix products, arithmetic and copies ran while one was open for 8% of the time, Pallas kernels for 0%

commit v1 on v0

--- a/solution.py
+++ b/solution.py
@@ -90,7 +90,18 @@
     )
     rows_self = lax.dynamic_slice_in_dim(w_self, col_start, col_count, 0)
     rows_neigh = lax.dynamic_slice_in_dim(w_neigh, col_start, col_count, 0)
-    neighbours_all = lax.all_gather(neighbours, "feat", axis=1, tiled=True)
+    ways = lax.axis_size("feat")
+    up = [(d, (d + 1) % ways) for d in range(ways)]
+    down = [(d, (d - 1) % ways) for d in range(ways)]
+    earlier_2, later = ([neighbours], [neighbours])
+    for _ in range(ways // 2):
+        earlier_2.append(lax.ppermute(earlier_2[-1], "feat", up))
+    for _ in range((ways - 1) // 2):
+        later.append(lax.ppermute(later[-1], "feat", down))
+    line = jnp.concatenate([*earlier_2[::-1], *later[1:]], axis=1)
+    neighbours_all = jnp.roll(
+        line, (lax.axis_index("feat") - ways // 2) * neighbours.shape[1], axis=1
+    )
     preact_all = (
         jnp.dot(feats_all, w_self, preferred_element_type=jnp.float32)
         + jnp.dot(neighbours_all, w_neigh, preferred_element_type=jnp.float32)

time: 414 us -> 417 us (level)
  blocking collectives: 13.4 us -> 0 us
  waiting for transfers between devices: 292 us -> 303 us
  starting transfers between devices: 47.4 us -> 55.6 us
    all_gather x1 -> x0, blocking collectives: 13.4 us -> none  [on_device(): neighbours_all = lax.all_gather(neighbours, 'feat', axis=1, tiled=True)]
    ppermute x0 -> x7, waiting for transfers between devices: none -> 9.4 us  [the longest x4 6.51 us: on_device(): earlier_2.append(lax.ppermute(earlier_2[-1], 'feat', up))]
    ppermute x0 -> x7, starting transfers between devices: none -> 8.97 us  [the longest x3 8.95 us: on_device(): later.append(lax.ppermute(later[-1], 'feat', down))]
  transfers between devices with their start and end apart: 9 -> 16, of which waited for: 5 -> 12; matrix products, arithmetic and copies ran while one was open for 8% -> 7% of each run, Pallas kernels for 0% -> 0%
where the time goes in v1:
time: 417 us; the launch traced here: 416 us
  waiting for transfers between devices  303 us (73%)
  starting transfers between devices  55.6 us (13%)
  local copies, waits for them, and re-layouts  20.6 us (5%)
  other arithmetic  15.3 us (4%)
  between operations  14.7 us (4%)
  matrix products  6.74 us (2%)
    psum x1, waiting for transfers between devices, on_device(): summed = lax.psum(slotted, ('rows', 'feat'))  266 us
    all_to_all x1, starting transfers between devices, on_device(): lax.all_to_all(request, 'rows', split_axis=0, concat_axis=0, tiled=True)  16.4 us
    ppermute x1, waiting for transfers between devices, extended(): lax.ppermute(lax.slice_in_dim(block, block.shape[dim] - width, None, axis...  13.9 us
    reshape x2, local copies, waits for them, and re-layouts, on_device(): returned.reshape(peer_count * capacity, tile_size * col_count)  10.3 us
    all_to_all x1, starting transfers between devices, on_device(): lax.all_to_all(returning.reshape(peer_count, capacity, tile_size, col_cou...  9.78 us
    ppermute x3, starting transfers between devices, on_device(): later.append(lax.ppermute(later[-1], 'feat', down))  8.95 us
  transfers between devices with their start and end apart: 16, of which 12 were waited for; matrix products, arithmetic and copies ran while one was open for 7% of the time, Pallas kernels for 0%

profile of v1, /device:TPU:24, one launch (start us, length us, event | category | flops | bytes accessed | tf_op | source)
XLA Modules:
  0.0 415.8 jit_solution(7628306227072923878)
XLA Ops:
  10.0 16.4 %all-to-all-start = ((s32[64,1,2]{2,1,0:T(1,128)}), s32[64,1,2]{2,1,0:T(1,128)S(1)}, u32[]{:S(2)}, u32[]{:S(2)}) async-start(s32[64,1,2]{2,1,0:T(1,128)} %bitcast.4), calls=%async_computation | async-start | bytes 65536 | tf_op jit(solution)/shard_map/all_to_all | solution.py:72
  26.3 0.9 copy_bitcast_fusion.4
  27.8 7.7 %all-to-all-done = s32[64,1,2]{2,1,0:T(1,128)S(1)} async-done(((s32[64,1,2]{2,1,0:T(1,128)}), s32[64,1,2]{2,1,0:T(1,128)S(1)}, u32[]{:S(2)}, u32[]{:S(2)}) %all-to-all-start) | async-done | bytes 544 | tf_op jit(solution)/shard_map/all_to_all | solution.py:72
  36.0 1.4 fusion.45
  38.7 1.2 broadcast_select_fusion
  39.8 7.3 %all-to-all-start.1 = ((bf16[64,2,128,32]{2,3,1,0:T(8,128)(2,1)}), bf16[64,2,128,32]{2,3,1,0:T(8,128)(2,1)S(1)}, u32[]{:S(2)}, u32[]{:S(2)}) async-start(bf16[64,2,128,32]{2,3,1,0:T(8,128)(2,1)} %broadcast_select_fusion), calls=%async_computation.1 | async-start | bytes 2097152 | tf_op jit(solution)/shard_map/all_to_all | solution.py:79
  48.0 4.6 %collective-permute-start = (bf16[128,32]{0,1:T(8,128)(2,1)S(1)}, bf16[128,32]{0,1:T(8,128)(2,1)S(1)}, u32[]{:S(2)}, u32[]{:S(2)}) collective-permute-start(bf16[128,32]{0,1:T(8,128)(2,1)S(1)} %get-tuple-element.51), channel_id=1, source_target_pairs={{0,8},{8,16},{16,24},{24,32},{32,40},{40,48},{48,56},{56,64},{64,7... | collective-permute-start | bytes 24584 | tf_op jit(solution)/shard_map/ppermute | solution.py:12
  52.6 1.9 collective-permute-start.1
  55.2 13.9 %collective-permute-done = bf16[128,32]{0,1:T(8,128)(2,1)S(1)} collective-permute-done((bf16[128,32]{0,1:T(8,128)(2,1)S(1)}, bf16[128,32]{0,1:T(8,128)(2,1)S(1)}, u32[]{:S(2)}, u32[]{:S(2)}) %collective-permute-start) | collective-permute-done | bytes 8224 | tf_op jit(solution)/shard_map/ppermute | solution.py:12
  69.1 2.1 collective-permute-done.1
  71.7 3.9 all-to-all-done.1
  76.6 4.9 %collective-permute-done.2 = bf16[1024,32]{0,1:T(8,128)(2,1)S(1)} collective-permute-done((bf16[1024,32]{0,1:T(8,128)(2,1)S(1)}, bf16[1024,32]{0,1:T(8,128)(2,1)S(1)}, u32[]{:S(2)}, u32[]{:S(2)}) %collective-permute-start.2) | collective-permute-done | bytes 65568 | tf_op jit(solution)/shard_map/ppermute | solution.py:98
  81.5 1.4 fusion.5
  82.9 3.0 collective-permute-start.6
  87.7 3.0 collective-permute-start.7
  91.5 1.1 collective-permute-done.7
  92.6 3.0 collective-permute-start.8
  96.3 1.3 collective-permute-done.8
  97.7 2.7 multiply_convert_fusion
  101.7 1.0 scatter_fusion
  102.8 1.2 convert_element_type.46
  104.0 9.8 %all-to-all-start.2 = ((bf16[64,2,128,32]{2,3,1,0:T(8,128)(2,1)}), bf16[64,2,128,32]{2,3,1,0:T(8,128)(2,1)S(1)}, u32[]{:S(2)}, u32[]{:S(2)}) async-start(bf16[64,2,128,32]{2,3,1,0:T(8,128)(2,1)} %bitcast.110), calls=%async_computation.2 | async-start | bytes 2097152 | tf_op jit(solution)/shard_map/all_to_all | solution.py:153
  115.8 1.6 multiply_convert_fusion.1
  117.4 4.6 %collective-permute-start.9 = (f32[128,32]{0,1:T(8,128)S(1)}, f32[128,32]{0,1:T(8,128)S(1)}, u32[]{:S(2)}, u32[]{:S(2)}) collective-permute-start(f32[128,32]{0,1:T(8,128)S(1)} %get-tuple-element.45), channel_id=1, source_target_pairs={{0,8},{8,16},{16,24},{24,32},{32,40},{40,48},{48,56},{56,64},{64,7... | collective-permute-start | bytes 49160 | tf_op jit(solution)/shard_map/ppermute | solution.py:23
  122.0 2.1 collective-permute-start.10
  124.8 265.7 %all-reduce.6.cloned.1.call-done = f32[2,8,32,256]{3,2,1,0:T(8,128)} async-done(((f32[2,8,32,256]{3,2,1,0:T(8,128)}), f32[2,8,32,256]{3,2,1,0:T(8,128)}) %all-reduce.6.cloned.1.call-update) | async-done | bytes 524304 | tf_op jit(solution)/shard_map/psum | solution.py:149
  390.5 1.4 fusion.28
  391.9 4.1 copy.120
  396.0 6.3 %reshape.303 = f32[128,4096]{1,0:T(8,128)S(1)} reshape(f32[64,2,128,32]{3,2,1,0:T(8,128)} %copy.120) | data formatting | bytes 4194304 | tf_op jit(solution)/shard_map/reshape | solution.py:163
  402.2 3.8 scatter_custom_fusion.1
  406.1 1.1 reshape.272
  407.3 0.9 fusion.1
  (130 shorter events, 16.1 us)
Async XLA Ops:
  7.2 90.5 %copy-start = (bf16[256,256]{1,0:T(8,128)(2,1)S(1)}, bf16[256,256]{1,0:T(8,128)(2,1)}, u32[]{:S(2)}) copy-start(bf16[256,256]{1,0:T(8,128)(2,1)} %param.21) | copy-start | bytes 393220
  10.0 25.6 %all-to-all-start = ((s32[64,1,2]{2,1,0:T(1,128)}), s32[64,1,2]{2,1,0:T(1,128)S(1)}, u32[]{:S(2)}, u32[]{:S(2)}) async-start(s32[64,1,2]{2,1,0:T(1,128)} %bitcast.4), calls=%async_computation | async-start | bytes 65536 | tf_op jit(solution)/shard_map/all_to_all | solution.py:72
  38.6 8.7 %copy-start.6 = (bf16[1024,32]{0,1:T(8,128)(2,1)S(1)}, bf16[1024,32]{0,1:T(8,128)(2,1)}, u32[]{:S(2)}) copy-start(bf16[1024,32]{0,1:T(8,128)(2,1)} %param.15) | copy-start | bytes 196612
  38.6 8.7 %copy-start.16 = (bf16[1024,32]{0,1:T(8,128)(2,1)S(1)}, bf16[1024,32]{0,1:T(8,128)(2,1)}, u32[]{:S(2)}) copy-start(bf16[1024,32]{0,1:T(8,128)(2,1)} %param.23) | copy-start | bytes 196612
  38.6 15.9 %copy-start.17 = (s32[8,2]{0,1:T(2,128)S(1)}, s32[8,2]{0,1:T(2,128)}, u32[]{:S(2)}) copy-start(s32[8,2]{0,1:T(2,128)} %param.18) | copy-start | bytes 196
  38.6 16.1 %copy-start.2 = (bf16[1024,256]{1,0:T(8,128)(2,1)S(1)}, bf16[1024,256]{1,0:T(8,128)(2,1)}, u32[]{:S(2)}) copy-start(bf16[1024,256]{1,0:T(8,128)(2,1)} %param.17) | copy-start | bytes 1572868
  38.6 16.3 %copy-start.1 = (bf16[1024,384]{1,0:T(8,128)(2,1)S(1)}, bf16[1024,384]{1,0:T(8,128)(2,1)}, u32[]{:S(2)}) copy-start(bf16[1024,384]{1,0:T(8,128)(2,1)} %param.16) | copy-start | bytes 2359300
  39.8 35.7 %all-to-all-start.1 = ((bf16[64,2,128,32]{2,3,1,0:T(8,128)(2,1)}), bf16[64,2,128,32]{2,3,1,0:T(8,128)(2,1)S(1)}, u32[]{:S(2)}, u32[]{:S(2)}) async-start(bf16[64,2,128,32]{2,3,1,0:T(8,128)(2,1)} %broadcast_select_fusion), calls=%async_computation.1 | async-start | bytes 2097152 | tf_op jit(solution)/shard_map/all_to_all | solution.py:79
  47.1 34.4 %all-gather.2.cloned.1.call-start = ((), (), s32[]{:S(2)}) async-start(), calls=%async_computation.3 | async-start | bytes 1253376 | tf_op jit(solution)/shard_map/all_gather | solution.py:44
  48.0 21.1 %collective-permute-start = (bf16[128,32]{0,1:T(8,128)(2,1)S(1)}, bf16[128,32]{0,1:T(8,128)(2,1)S(1)}, u32[]{:S(2)}, u32[]{:S(2)}) collective-permute-start(bf16[128,32]{0,1:T(8,128)(2,1)S(1)} %get-tuple-element.51), channel_id=1, source_target_pairs={{0,8},{8,16},{16,24},{24,32},{32,40},{40,48},{48,56},{56,64},{64,7... | collective-permute-start | bytes 24584 | tf_op jit(solution)/shard_map/ppermute | solution.py:12
  52.6 18.7 %collective-permute-start.1 = (bf16[128,32]{0,1:T(8,128)(2,1)S(1)}, bf16[128,32]{0,1:T(8,128)(2,1)S(1)}, u32[]{:S(2)}, u32[]{:S(2)}) collective-permute-start(bf16[128,32]{0,1:T(8,128)(2,1)S(1)} %get-tuple-element.52), channel_id=1, source_target_pairs={{8,0},{16,8},{24,16},{32,24},{40,32},{48,40},{56,48},{64,56},{72,6... | collective-permute-start | bytes 24584 | tf_op jit(solution)/shard_map/ppermute | solution.py:15
  71.3 10.2 %copy-start.14 = (bf16[256,256]{1,0:T(8,128)(2,1)S(1)}, bf16[256,256]{1,0:T(8,128)(2,1)}, u32[]{:S(2)}) copy-start(bf16[256,256]{1,0:T(8,128)(2,1)} %param.20) | copy-start | bytes 393220
  76.6 21.1 %copy-start.9 = (bf16[1024,32]{0,1:T(8,128)(2,1)}, bf16[1024,32]{0,1:T(8,128)(2,1)S(1)}, u32[]{:S(2)}) copy-start(bf16[1024,32]{0,1:T(8,128)(2,1)S(1)} %fusion.16) | copy-start | bytes 196612
  76.6 4.9 %collective-permute-start.2 = (bf16[1024,32]{0,1:T(8,128)(2,1)S(1)}, bf16[1024,32]{0,1:T(8,128)(2,1)S(1)}, u32[]{:S(2)}, u32[]{:S(2)}) collective-permute-start(bf16[1024,32]{0,1:T(8,128)(2,1)S(1)} %fusion.16), channel_id=1, source_target_pairs={{0,1},{1,2},{2,3},{3,4},{4,5},{5,6},{6,7},{7,0},{8,9},{9,10},{10,1... | collective-permute-start | bytes 196616 | tf_op jit(solution)/shard_map/ppermute | solution.py:98
  81.5 4.9 %collective-permute-start.3 = (bf16[1024,32]{0,1:T(8,128)(2,1)S(1)}, bf16[1024,32]{0,1:T(8,128)(2,1)S(1)}, u32[]{:S(2)}, u32[]{:S(2)}) collective-permute-start(bf16[1024,32]{0,1:T(8,128)(2,1)S(1)} %collective-permute-done.2), channel_id=1, source_target_pairs={{0,1},{1,2},{2,3},{3,4},{4,5},{5,6},{6,7},{7,0},{8,9},{9,10},{10,1... | collective-permute-start | bytes 196616 | tf_op jit(solution)/shard_map/ppermute | solution.py:98
  82.9 4.9 %collective-permute-start.6 = (bf16[1024,32]{0,1:T(8,128)(2,1)S(1)}, bf16[1024,32]{0,1:T(8,128)(2,1)S(1)}, u32[]{:S(2)}, u32[]{:S(2)}) collective-permute-start(bf16[1024,32]{0,1:T(8,128)(2,1)S(1)} %fusion.16), channel_id=1, source_target_pairs={{0,7},{1,0},{2,1},{3,2},{4,3},{5,4},{6,5},{7,6},{8,15},{9,8},{10,9... | collective-permute-start | bytes 196616 | tf_op jit(solution)/shard_map/ppermute | solution.py:100
  86.4 4.9 %collective-permute-start.4 = (bf16[1024,32]{0,1:T(8,128)(2,1)S(1)}, bf16[1024,32]{0,1:T(8,128)(2,1)S(1)}, u32[]{:S(2)}, u32[]{:S(2)}) collective-permute-start(bf16[1024,32]{0,1:T(8,128)(2,1)S(1)} %collective-permute-done.3), channel_id=1, source_target_pairs={{0,1},{1,2},{2,3},{3,4},{4,5},{5,6},{6,7},{7,0},{8,9},{9,10},{10,1... | collective-permute-start | bytes 196616 | tf_op jit(solution)/shard_map/ppermute | solution.py:98
  87.7 4.9 %collective-permute-start.7 = (bf16[1024,32]{0,1:T(8,128)(2,1)S(1)}, bf16[1024,32]{0,1:T(8,128)(2,1)S(1)}, u32[]{:S(2)}, u32[]{:S(2)}) collective-permute-start(bf16[1024,32]{0,1:T(8,128)(2,1)S(1)} %collective-permute-done.6), channel_id=1, source_target_pairs={{0,7},{1,0},{2,1},{3,2},{4,3},{5,4},{6,5},{7,6},{8,15},{9,8},{10,9... | collective-permute-start | bytes 196616 | tf_op jit(solution)/shard_map/ppermute | solution.py:100
  91.3 4.9 %collective-permute-start.5 = (bf16[1024,32]{0,1:T(8,128)(2,1)S(1)}, bf16[1024,32]{0,1:T(8,128)(2,1)S(1)}, u32[]{:S(2)}, u32[]{:S(2)}) collective-permute-start(bf16[1024,32]{0,1:T(8,128)(2,1)S(1)} %collective-permute-done.4), channel_id=1, source_target_pairs={{0,1},{1,2},{2,3},{3,4},{4,5},{5,6},{6,7},{7,0},{8,9},{9,10},{10,1... | collective-permute-start | bytes 196616 | tf_op jit(solution)/shard_map/ppermute | solution.py:98
  92.6 4.9 %collective-permute-start.8 = (bf16[1024,32]{0,1:T(8,128)(2,1)S(1)}, bf16[1024,32]{0,1:T(8,128)(2,1)S(1)}, u32[]{:S(2)}, u32[]{:S(2)}) collective-permute-start(bf16[1024,32]{0,1:T(8,128)(2,1)S(1)} %collective-permute-done.7), channel_id=1, source_target_pairs={{0,7},{1,0},{2,1},{3,2},{4,3},{5,4},{6,5},{7,6},{8,15},{9,8},{10,9... | collective-permute-start | bytes 196616 | tf_op jit(solution)/shard_map/ppermute | solution.py:100
  100.4 0.8 copy-start.3
  104.0 9.9 %copy-start.15 = (s32[64,2]{1,0:T(8,128)S(1)}, s32[64,2]{1,0:T(8,128)}, u32[]{:S(2)}) copy-start(s32[64,2]{1,0:T(8,128)} %get-tuple-element.40) | copy-start | bytes 1540
  104.0 10.0 %copy-start.12 = (bf16[4,8,8,128]{3,2,1,0:T(8,128)(2,1)S(1)}, bf16[4,8,8,128]{3,2,1,0:T(8,128)(2,1)}, u32[]{:S(2)}) copy-start(bf16[4,8,8,128]{3,2,1,0:T(8,128)(2,1)} %copy-done.11) | copy-start | bytes 196612
  104.0 10.4 %copy-start.4 = (bf16[1024,256]{0,1:T(8,128)(2,1)S(1)}, bf16[1024,256]{0,1:T(8,128)(2,1)}, u32[]{:S(2)}) copy-start(bf16[1024,256]{0,1:T(8,128)(2,1)} %copy-done.3) | copy-start | bytes 1572868
  104.0 10.4 %copy-start.10 = (bf16[1024,32]{0,1:T(8,128)(2,1)S(1)}, bf16[1024,32]{0,1:T(8,128)(2,1)}, u32[]{:S(2)}) copy-start(bf16[1024,32]{0,1:T(8,128)(2,1)} %copy-done.9) | copy-start | bytes 196612
  104.0 287.9 %all-to-all-start.2 = ((bf16[64,2,128,32]{2,3,1,0:T(8,128)(2,1)}), bf16[64,2,128,32]{2,3,1,0:T(8,128)(2,1)S(1)}, u32[]{:S(2)}, u32[]{:S(2)}) async-start(bf16[64,2,128,32]{2,3,1,0:T(8,128)(2,1)} %bitcast.110), calls=%async_computation.2 | async-start | bytes 2097152 | tf_op jit(solution)/shard_map/all_to_all | solution.py:153
  113.8 0.9 copy-start.7
  113.8 276.7 %all-reduce.6.cloned.1.call-start = ((), (), s32[]{:S(2)}) async-start(), calls=%async_computation.4 | async-start | bytes 1048576 | tf_op jit(solution)/shard_map/psum | solution.py:149
  115.0 0.8 copy-start.5
  117.4 290.9 %collective-permute-start.9 = (f32[128,32]{0,1:T(8,128)S(1)}, f32[128,32]{0,1:T(8,128)S(1)}, u32[]{:S(2)}, u32[]{:S(2)}) collective-permute-start(f32[128,32]{0,1:T(8,128)S(1)} %get-tuple-element.45), channel_id=1, source_target_pairs={{0,8},{8,16},{16,24},{24,32},{32,40},{40,48},{48,56},{56,64},{64,7... | collective-permute-start | bytes 49160 | tf_op jit(solution)/shard_map/ppermute | solution.py:23
  122.0 286.3 %collective-permute-start.10 = (f32[128,32]{0,1:T(8,128)S(1)}, f32[128,32]{0,1:T(8,128)S(1)}, u32[]{:S(2)}, u32[]{:S(2)}) collective-permute-start(f32[128,32]{0,1:T(8,128)S(1)} %get-tuple-element.44), channel_id=1, source_target_pairs={{8,0},{16,8},{24,16},{32,24},{40,32},{48,40},{56,48},{64,56},{72,6... | collective-permute-start | bytes 49160 | tf_op jit(solution)/shard_map/ppermute | solution.py:23
  396.0 11.3 %copy-start.8 = (f32[1280,32]{0,1:T(8,128)S(1)}, f32[1280,32]{0,1:T(8,128)}, u32[]{:S(2)}) copy-start(f32[1280,32]{0,1:T(8,128)} %pad_add_fusion) | copy-start | bytes 491524
  (2 other events, 1.3 us)
Sparse Core Ops, SparseCore 0:
  50.1 29.6 all-gather.1
  119.6 270.8 all-reduce.5
